TPU v7x, 32 devices: a whole 2x2x4 slice. The times are simulated.
32 devices in a mesh: req: 4 (over y, x), head: 4 (over z), dev: 2 (over core).
Axes of the slice: x: 2, y: 2, z: 4, core: 2. Of those that a mesh axis runs over, the one named last changes fastest.
Arguments:
- tokens: bfloat16 [4, 512, 2304], P('req', 'dev')
- attn_gain: float32 [2304], replicated, may hold values from 0.1 to 1.9
- w_qkv: bfloat16 [2304, 3, 2048], P(None, None, 'head')
- w_out: bfloat16 [2048, 2304], P('head'), may hold values from -0.125 to 0.125
- moe_gain: float32 [2304], replicated, may hold values from 0.1 to 1.9
- routes: int32 [4, 512, 2], P(None, 'dev'), may hold values from 0 to 7, all different within a row; in each aligned block of 256 rows (0 to 255, 256 to 511, ..., all dimensions but the last counted through in order) at most 96 rows name the same one
- route_weight: float32 [4, 512, 2], P(None, 'dev'), may hold values from 0.2 to 1
- w_gate_up: bfloat16 [8, 2, 2304, 5760], P('head', None, None, 'req'), may hold values from -0.125 to 0.125
- w_down: bfloat16 [8, 5760, 2304], P('head', 'req'), may hold values from -0.078125 to 0.078125
- kv_cache: bfloat16 [4, 16, 128, 2, 2048], P('req', None, 'dev', None, 'head'), may hold values from -6 to 6
- lengths: int32 [4], replicated, may hold values from 1 to 2048, as said below
- block_owner: int32 [4, 16], replicated, may hold values from 0 to 3, as said below
- block_slot: int32 [4, 16], replicated, may hold values from 0 to 15, as said below
Outputs:
- layer_out: bfloat16 [4, 2, 256, 2304], P('req', 'dev', 'head')
- page_pool: bfloat16 [64, 128, 2, 2048], P('req', 'dev', None, 'head')
Inputs may be any that keep to these rules, and one draw needn't show every extreme that they name: `routes`: in each aligned block of 256 rows (the rows of one device) no expert is named more than 96 times; the other loads are skewed. `lengths`: each request has a length of 1 or more tokens; some request has exactly 2048. `block_owner`: each holder holds exactly 4 pages of every request. The pairs of block_owner and block_slot are distinct over all pages of all requests.
All inputs are finite; a program needn't handle non-finite values.
Results may differ from a plain program's by a relative error of at most 0.012.
Values may be sent and summed in bfloat16 or wider, within the bound.
No kernel may reach another device: no remote copies, remote signals or barrier semaphores. Data moves between devices by JAX's collectives and lax.ppermute only.
A program may use at most 192 MiB of HBM per device.

v0:
```python
import jax
import jax.numpy as jnp
from jax import lax
from jax.sharding import PartitionSpec as P

EXPERTS = 8
HD = 64


def shifted(block, axis, distance):
    devices = range(lax.axis_size(axis))
    route = [(i - distance, i) for i in devices if i - distance in devices]
    return lax.ppermute(block, axis, route)


def norm_rows(values, gain_vec):
    widened = values.astype(jnp.float32)
    inv_rms = lax.rsqrt(jnp.mean(widened * widened, axis=-1, keepdims=True) + 1e-05)
    return (widened * inv_rms * gain_vec).astype(jnp.bfloat16)


def rotate(values, positions):
    half_dim = values.shape[-1] // 2
    frequency = 10000.0 ** (-jnp.arange(half_dim, dtype=jnp.float32) / half_dim)
    angles = positions[:, None] * frequency[None, :]
    cosine = jnp.cos(angles)[:, None, :]
    sine_part = jnp.sin(angles)[:, None, :]
    front_half = values[..., :half_dim]
    back_half = values[..., half_dim:]
    return jnp.concatenate(
        [front_half * cosine - back_half * sine_part, back_half * cosine + front_half * sine_part],
        axis=-1,
    )


def slot_tables(route_ids, weights, first_expert, experts_here, capacity):
    expert_ids = first_expert + jnp.arange(experts_here, dtype=jnp.int32)
    matches = (route_ids[..., None] == expert_ids).astype(jnp.float32)
    hit_shape = matches.shape
    flat_hits = matches.reshape(hit_shape[:-3] + (hit_shape[-3] * hit_shape[-2], hit_shape[-1]))
    ranking = (jnp.cumsum(flat_hits, axis=-2) - flat_hits).reshape(hit_shape)
    places = (ranking[..., None] == jnp.arange(capacity, dtype=jnp.float32)).astype(
        jnp.float32
    ) * matches[..., None]
    dispatch = jnp.sum(places, axis=-3)
    combine = jnp.sum(places * weights[..., None, None], axis=-3)
    return (dispatch, combine)


def body(
    tokens,
    attn_gain,
    w_qkv,
    w_out,
    moe_gain,
    routes,
    route_weight,
    w_gate_up,
    w_down,
    kv_cache,
    lengths,
    block_owner,
    block_slot,
):
    half_rows = tokens.shape[1]
    model_width = tokens.shape[2]
    dev_index = lax.axis_index("dev")
    req_index = lax.axis_index("req")
    head_index = lax.axis_index("head")
    local_cols = w_qkv.shape[2]
    head_count = local_cols // HD
    normed = norm_rows(tokens[0], attn_gain)
    projected = jnp.dot(
        normed, w_qkv.reshape(model_width, 3 * local_cols), preferred_element_type=jnp.float32
    ).reshape(half_rows, 3, head_count, HD)
    query_pos = dev_index * half_rows + jnp.arange(half_rows, dtype=jnp.int32)
    angles_at = query_pos.astype(jnp.float32)
    queries = rotate(projected[:, 0], angles_at).astype(jnp.bfloat16)
    key_rows = rotate(projected[:, 1], angles_at).astype(jnp.bfloat16)
    values = projected[:, 2].astype(jnp.bfloat16)
    earlier_keys, earlier_values = shifted((key_rows, values), "dev", 1)
    all_keys = jnp.concatenate([earlier_keys, key_rows], axis=0)
    all_values = jnp.concatenate([earlier_values, values], axis=0)
    key_pos = (dev_index - 1) * half_rows + jnp.arange(2 * half_rows, dtype=jnp.int32)
    allowed = (key_pos[None, :] <= query_pos[:, None]) & (key_pos[None, :] >= 0)
    scores = (
        jnp.einsum("qhd,khd->hqk", queries, all_keys, preferred_element_type=jnp.float32) * 0.125
    )
    scores = jnp.where(allowed[None], scores, -1e30)
    row_peak = jnp.max(scores, axis=-1, keepdims=True)
    exp_scores = jnp.exp(scores - row_peak)
    row_total = jnp.sum(exp_scores, axis=-1)
    attended = (
        jnp.einsum(
            "hqk,khd->qhd",
            exp_scores.astype(jnp.bfloat16),
            all_values,
            preferred_element_type=jnp.float32,
        )
        / jnp.transpose(row_total)[:, :, None]
    )
    attended = attended.astype(jnp.bfloat16).reshape(half_rows, local_cols)
    partial_value = jnp.dot(attended, w_out, preferred_element_type=jnp.float32)
    attn_mixed = lax.psum(partial_value.astype(jnp.bfloat16), "head").astype(jnp.float32)
    residual = (tokens[0].astype(jnp.float32) + attn_mixed).astype(jnp.bfloat16)
    moe_in = norm_rows(residual, moe_gain)
    experts_here = w_gate_up.shape[0]
    first_expert = head_index * experts_here
    top_count = routes.shape[2]
    capacity = half_rows * top_count * 3 // (2 * EXPERTS)
    own_routes = lax.dynamic_index_in_dim(routes, req_index, 0, keepdims=True)
    own_weights = lax.dynamic_index_in_dim(route_weight, req_index, 0, keepdims=True)
    own_dispatch, own_combine = slot_tables(
        own_routes, own_weights, first_expert, experts_here, capacity
    )
    own_dispatch = own_dispatch[0]
    own_combine = own_combine[0]
    picked_own = jnp.einsum(
        "tec,td->ced", own_dispatch.astype(jnp.bfloat16), moe_in, preferred_element_type=jnp.float32
    ).astype(jnp.bfloat16)
    req_total = lax.axis_size("req")
    dev_total = lax.axis_size("dev")
    split = dev_total > 1 and experts_here % dev_total == 0
    per_core = experts_here // dev_total if split else experts_here
    if split:
        first_here = dev_index * per_core
        gate_up_here = lax.dynamic_slice_in_dim(w_gate_up, first_here, per_core, 0)
        down_here = lax.dynamic_slice_in_dim(w_down, first_here, per_core, 0)
        rows_here = lax.all_to_all(picked_own, "dev", split_axis=1, concat_axis=0, tiled=True)
    else:
        gate_up_here, down_here, rows_here = (w_gate_up, w_down, picked_own)

    def partner_move(block, step):
        return lax.ppermute(block, "req", [(i, i ^ step) for i in range(req_total)])

    def experts_on(rows):
        groups = rows.shape[0]
        flat = rows.reshape(groups * rows.shape[1], per_core, model_width)
        both = jnp.einsum("ned,egdf->gnef", flat, gate_up_here, preferred_element_type=jnp.float32)
        hidden = (jax.nn.silu(both[0]) * both[1]).astype(jnp.bfloat16)
        down = jnp.einsum("nef,efd->ned", hidden, down_here, preferred_element_type=jnp.float32)
        return down.astype(jnp.bfloat16).reshape(rows.shape)

    arrived = {0: rows_here}
    for step in range(1, req_total):
        if step == 3:
            arrived[step] = partner_move(arrived[1], 2)
        else:
            arrived[step] = partner_move(rows_here, step)
    plan = [[0], [1, 2]] + ([list(range(3, req_total))] if req_total > 3 else [])
    plan = [[k for k in group if k < req_total] for group in plan]
    returned = []
    for group in plan:
        if not group:
            continue
        outs = experts_on(jnp.stack([arrived[k] for k in group], axis=0))
        for slot_index, step in enumerate(group):
            part = outs[slot_index]
            part = part if step == 0 else partner_move(part, step)
            if split:
                part = lax.all_to_all(part, "dev", split_axis=0, concat_axis=1, tiled=True)
            returned.append(part)
    token_weights = jnp.sum(own_combine, axis=-1)
    dispatch_bf = own_dispatch.astype(jnp.bfloat16)
    selected = sum(
        (
            jnp.einsum("tec,ced->ted", dispatch_bf, part, preferred_element_type=jnp.float32)
            for part in returned
        )
    )
    moe_out = jnp.sum(token_weights[:, :, None] * selected, axis=1)
    summed = lax.psum_scatter(
        moe_out.astype(jnp.bfloat16), "head", scatter_dimension=0, tiled=True
    ).astype(jnp.float32)
    rows_out = summed.shape[0]
    kept_rows = lax.dynamic_slice_in_dim(residual, head_index * rows_out, rows_out, 0)
    layer_out = (
        (kept_rows.astype(jnp.float32) + summed)
        .astype(jnp.bfloat16)
        .reshape(1, 1, rows_out, model_width)
    )
    owners_total = lax.axis_size("req")
    block_total = block_owner.shape[1]
    finished_total = block_owner.shape[0]
    per_owner = block_total // owners_total
    block_ids = jnp.arange(block_total, dtype=jnp.int32)
    same_owner = block_owner[:, :, None] == block_owner[:, None, :]
    before_mask = block_ids[None, :] < block_ids[:, None]
    page_rank = jnp.sum((same_owner & before_mask[None]).astype(jnp.int32), axis=2)
    own_owner = lax.dynamic_index_in_dim(block_owner, req_index, 0, keepdims=False)
    own_rank = lax.dynamic_index_in_dim(page_rank, req_index, 0, keepdims=False)
    dest_place = own_owner * per_owner + own_rank
    source_block = jnp.sum(
        jnp.where(dest_place[None, :] == block_ids[:, None], block_ids[None, :], 0), axis=1
    )
    page_half = kv_cache.shape[2]
    page_size = page_half * lax.axis_size("dev")
    token_pos = (
        block_ids[:, None] * page_size
        + dev_index * page_half
        + jnp.arange(page_half, dtype=jnp.int32)[None, :]
    )
    own_length = lax.dynamic_index_in_dim(lengths, req_index, 0, keepdims=False)
    live_cache = jnp.where(
        (token_pos < own_length)[:, :, None, None], kv_cache[0], jnp.zeros((), jnp.bfloat16)
    )
    outgoing = jnp.take(live_cache, source_block, axis=0)
    received = lax.all_to_all(outgoing, "req", split_axis=0, concat_axis=0, tiled=True)
    request_ids = jnp.arange(finished_total, dtype=jnp.int32)
    arrive_place = request_ids[:, None] * per_owner + page_rank
    own_blocks = block_owner == req_index
    slot_match = own_blocks[None] & (block_slot[None] == block_ids[:, None, None])
    gather_place = jnp.sum(jnp.where(slot_match, arrive_place[None], 0), axis=(1, 2))
    page_pool = jnp.take(received, gather_place, axis=0)
    return (layer_out, page_pool)


def solution(mesh):
    return jax.shard_map(
        body,
        mesh=mesh,
        in_specs=(
            P("req", "dev", None),
            P(),
            P(None, None, "head"),
            P("head", None),
            P(),
            P(None, "dev", None),
            P(None, "dev", None),
            P("head", None, None, "req"),
            P("head", "req", None),
            P("req", None, "dev", None, "head"),
            P(),
            P(),
            P(),
        ),
        out_specs=(P("req", "dev", "head", None), P("req", "dev", None, "head")),
        check_vma=False,
    )
```

profile of v0, /device:TPU:0, one launch (start us, length us, event | category | flops | bytes accessed | tf_op | source)
XLA Modules:
  0.0 311.2 jit_solution(5563176906753510006)
XLA Ops:
  7.3 9.9 %copy.53 = bf16[2304,3,512]{0,2,1:T(8,128)(2,1)} copy(bf16[2304,3,512]{2,0,1:T(8,128)(2,1)} %param.17) | data formatting | bytes 14155776 | tf_op args[2]
  17.5 5.2 %fusion.68 = f32[256,3,8,64]{0,3,2,1:T(8,128)S(1)} fusion(bf16[3,8,64,2304]{3,2,1,0:T(8,128)(2,1)} %bitcast.186, bf16[1,256,2304]{2,1,0:T(8,128)(2,1)S(1)} %copy-done.2, f32[2304]{0:T(1024)} %param.16, f32[256]{0:T(256)S(1)} %add_rsqrt_fusion.1), kind=kOutput, calls=%fused_computation.64 | convolution fusion | flops 1814298624 | bytes 9840640 | tf_op jit(solution)/shard_map/dot_general | solution.py:73
  23.2 3.1 collective-permute-start.1
  26.2 2.0 collective-permute-start
  30.6 1.9 fusion.35
  33.8 2.2 fusion.83
  35.9 1.8 convolution_convert_fusion
  40.7 55.2 %all-reduce.2.cloned.1.call-done = bf16[256,2304]{1,0:T(8,128)(2,1)} async-done(((bf16[256,2304]{1,0:T(8,128)(2,1)}), bf16[256,2304]{1,0:T(8,128)(2,1)}) %all-reduce.2.cloned.1.call-update) | async-done | bytes 1179664 | tf_op jit(solution)/shard_map/psum | solution.py:104
  95.9 1.8 fusion.52
  98.4 5.4 %all_to_all.95 = bf16[96,2,2304]{2,0,1:T(8,128)(2,1)} all-to-all(bf16[96,2,2304]{2,0,1:T(8,128)(2,1)S(1)} %convert_bitcast_fusion.1), channel_id=1, replica_groups=mesh['req'=4,'head'=4,'dev'=2] {'dev'}, dimensions={1} | all-to-all | bytes 1769472 | tf_op jit(solution)/shard_map/all_to_all | solution.py:129
  109.1 2.3 gather_fusion
  111.3 14.4 %collective-permute-done.2 = bf16[192,1,2304]{2,0,1:T(8,128)(2,1)} collective-permute-done((bf16[192,1,2304]{2,0,1:T(8,128)(2,1)}, bf16[192,1,2304]{2,0,1:T(8,128)(2,1)}, u32[]{:S(2)}, u32[]{:S(2)}) %collective-permute-start.2) | collective-permute-done | bytes 884768 | tf_op jit(solution)/shard_map/ppermute | solution.py:134
  127.0 1.7 pad_maximum_fusion
  128.8 9.9 %fusion.26 = f32[2,384,1,1440]{1,3,0,2:T(8,128)S(1)} fusion(bf16[384,2304,1]{1,0,2:T(8,128)(2,1)S(1)} %bitcast.193, bf16[2,2,2304,1440]{2,3,1,0:T(8,128)(2,1)} %param.22, s32[]{:T(128)S(6)} %select_n.44), kind=kOutput, calls=%fused_computation.30 | convolution fusion | flops 5096079360 | bytes 19464196 | tf_op jit(solution)/shard_map/ned,egdf->gnef/dot_general | solution.py:139
  138.7 3.0 fusion.23
  145.7 7.6 %fusion.44 = f32[2,192,1,1440]{3,1,0,2:T(8,128)S(1)} fusion(bf16[192,2304,1]{1,0,2:T(8,128)(2,1)} %bitcast.26, bf16[2,2,2304,1440]{2,3,1,0:T(8,128)(2,1)} %param.22, s32[]{:T(128)S(6)} %select_n.44), kind=kOutput, calls=%fused_computation.38 | convolution fusion | flops 2548039680 | bytes 16367620 | tf_op jit(solution)/shard_map/ned,egdf->gnef/dot_general | solution.py:139
  153.3 2.6 fusion.36
  156.4 3.1 %reduce.7 = bf16[192,2304]{1,0:T(8,128)(2,1)} reduce(bf16[192,1,2304]{2,0,1:T(8,128)(2,1)} %fusion.36, bf16[]{:T(256)} %broadcast.399), dimensions={1}, to_apply=%copy.56.reduce_sub_computation | reduce | bytes 1769474 | tf_op jit(solution)/shard_map/convert_element_type | solution.py:142
  159.5 2.0 reshape.485
  161.5 6.4 %all_to_all.96 = bf16[2,2,110592]{2,1,0:T(2,128)(2,1)} all-to-all(bf16[2,2,110592]{2,1,0:T(2,128)(2,1)} %reshape.485), channel_id=1, replica_groups=mesh['req'=4,'head'=4,'dev'=2] {'dev'}, dimensions={0} | all-to-all | bytes 1769472 | tf_op jit(solution)/shard_map/all_to_all | solution.py:161
  168.0 2.7 reshape.486
  172.2 3.0 fusion.128
  175.2 3.1 %reduce.8 = bf16[192,2304]{1,0:T(8,128)(2,1)} reduce(bf16[192,1,2304]{2,0,1:T(8,128)(2,1)} %collective-permute-done.4, bf16[]{:T(256)} %broadcast.399), dimensions={1}, to_apply=%copy.57.reduce_sub_computation | reduce | bytes 1769474 | tf_op jit(solution)/shard_map/ppermute | solution.py:134
  178.3 2.1 reshape.487
  180.4 6.5 %all_to_all.97 = bf16[2,2,110592]{2,1,0:T(2,128)(2,1)} all-to-all(bf16[2,2,110592]{2,1,0:T(2,128)(2,1)} %reshape.487), channel_id=1, replica_groups=mesh['req'=4,'head'=4,'dev'=2] {'dev'}, dimensions={0} | all-to-all | bytes 1769472 | tf_op jit(solution)/shard_map/all_to_all | solution.py:161
  186.9 2.7 reshape.488
  189.6 2.5 copy.65
  192.1 3.1 %reduce.9 = bf16[192,2304]{1,0:T(8,128)(2,1)} reduce(bf16[192,1,2304]{2,0,1:T(8,128)(2,1)} %collective-permute-done.5, bf16[]{:T(256)} %broadcast.399), dimensions={1}, to_apply=%copy.58.reduce_sub_computation | reduce | bytes 1769474 | tf_op jit(solution)/shard_map/ppermute | solution.py:134
  195.2 2.1 reshape.489
  197.3 6.4 %all_to_all.98 = bf16[2,2,110592]{2,1,0:T(2,128)(2,1)} all-to-all(bf16[2,2,110592]{2,1,0:T(2,128)(2,1)} %reshape.489), channel_id=1, replica_groups=mesh['req'=4,'head'=4,'dev'=2] {'dev'}, dimensions={0} | all-to-all | bytes 1769472 | tf_op jit(solution)/shard_map/all_to_all | solution.py:161
  203.7 2.7 reshape.490
  206.4 1.7 copy.66
  208.2 8.4 %fusion.47 = f32[2,192,1,1440]{3,1,0,2:T(8,128)S(1)} fusion(bf16[2,2,2304,1440]{2,3,1,0:T(8,128)(2,1)} %param.22, s32[]{:T(128)S(6)} %select_n.44, bf16[192,1,2304]{2,0,1:T(8,128)(2,1)} %collective-permute-done.6), kind=kOutput, calls=%fused_computation.39 | convolution fusion | flops 2548039680 | bytes 16367620 | tf_op jit(solution)/shard_map/ned,egdf->gnef/dot_general | solution.py:139
  218.9 2.5 collective-permute-start.7
  222.1 3.0 convolution_add_fusion.1
  225.1 16.5 %collective-permute-done.7 = bf16[192,1,2304]{2,0,1:T(8,128)(2,1)} collective-permute-done((bf16[192,1,2304]{2,0,1:T(8,128)(2,1)S(1)}, bf16[192,1,2304]{2,0,1:T(8,128)(2,1)}, u32[]{:S(2)}, u32[]{:S(2)}) %collective-permute-start.7) | collective-permute-done | bytes 884768 | tf_op jit(solution)/shard_map/ppermute | solution.py:134
  241.6 3.1 %reduce.10 = bf16[192,2304]{1,0:T(8,128)(2,1)} reduce(bf16[192,1,2304]{2,0,1:T(8,128)(2,1)} %collective-permute-done.7, bf16[]{:T(256)} %broadcast.399), dimensions={1}, to_apply=%copy.59.reduce_sub_computation | reduce | bytes 1769474 | tf_op jit(solution)/shard_map/ppermute | solution.py:134
  244.7 2.0 reshape.491
  246.8 6.4 %all_to_all.99 = bf16[2,2,110592]{2,1,0:T(2,128)(2,1)} all-to-all(bf16[2,2,110592]{2,1,0:T(2,128)(2,1)} %reshape.491), channel_id=1, replica_groups=mesh['req'=4,'head'=4,'dev'=2] {'dev'}, dimensions={0} | all-to-all | bytes 1769472 | tf_op jit(solution)/shard_map/all_to_all | solution.py:161
  253.2 2.7 reshape.492
  257.5 4.5 %fusion.63 = bf16[256,2304]{0,1:T(8,128)(2,1)} fusion(f32[2,2304,256]{2,1,0:T(8,128)} %convolution_add_fusion.1, bf16[96,2,2304]{2,0,1:T(8,128)(2,1)S(1)} %bitcast.191, bf16[256,2,96]{0,2,1:T(8,128)(2,1)S(1)} %get-tuple-element.14, f32[256,2]{0,1:T(2,128)S(1)} %get-tuple-element.13), kind=kOutput, calls=%fused_computation.60 | convolution fusion | flops 229441536 | bytes 6883328 | tf_op jit(solution)/shard_map/tec,ced->ted/dot_general | solution.py:167
  262.0 2.4 copy.60
  266.0 3.8 %all-to-all-start.5 = ((bf16[16,64,2,512]{3,1,2,0:T(8,128)(2,1)}), bf16[16,64,2,512]{3,1,2,0:T(8,128)(2,1)S(1)}, u32[]{:S(2)}, u32[]{:S(2)}) async-start(bf16[16,64,2,512]{3,1,2,0:T(8,128)(2,1)} %broadcast_select_fusion.1), calls=%async_computation.6 | async-start | bytes 4194304 | tf_op jit(solution)/shard_map/all_to_all | solution.py:208
  270.0 25.1 %all-to-all-done.5 = bf16[16,64,2,512]{3,1,2,0:T(8,128)(2,1)S(1)} async-done(((bf16[16,64,2,512]{3,1,2,0:T(8,128)(2,1)}), bf16[16,64,2,512]{3,1,2,0:T(8,128)(2,1)S(1)}, u32[]{:S(2)}, u32[]{:S(2)}) %all-to-all-start.5) | async-done | bytes 2097184 | tf_op jit(solution)/shard_map/all_to_all | solution.py:208
  295.1 2.0 gather_fusion.1
  297.1 2.0 broadcast_select_fusion
  299.1 3.5 %copy.62 = bf16[16,64,2,512]{3,2,1,0:T(2,128)(2,1)} copy(bf16[16,64,2,512]{3,1,2,0:T(8,128)(2,1)S(1)} %broadcast_select_fusion) | data formatting | bytes 4194304
  302.6 1.7 fusion.101
  (121 shorter events, 27.1 us)
Async XLA Ops:
  7.2 28.7 %copy-start = (bf16[512,2304]{1,0:T(8,128)(2,1)S(1)}, bf16[512,2304]{1,0:T(8,128)(2,1)}, u32[]{:S(2)}) copy-start(bf16[512,2304]{1,0:T(8,128)(2,1)} %param.18) | copy-start | bytes 7077892
  7.2 88.7 %all-reduce.2.cloned.1.call-start = ((), (), s32[]{:S(2)}) async-start(), calls=%async_computation.7 | async-start | bytes 2359296 | tf_op jit(solution)/shard_map/psum | solution.py:104
  7.3 9.9 %copy-start.2 = (bf16[1,256,2304]{2,1,0:T(8,128)(2,1)S(1)}, bf16[1,256,2304]{2,1,0:T(8,128)(2,1)}, u32[]{:S(2)}) copy-start(bf16[1,256,2304]{2,1,0:T(8,128)(2,1)} %param.15) | copy-start | bytes 3538948
  23.2 7.4 %collective-permute-start.1 = (bf16[256,8,64]{0,2,1:T(8,128)(2,1)S(1)}, bf16[256,8,64]{0,2,1:T(8,128)(2,1)}, u32[]{:S(2)}, u32[]{:S(2)}) collective-permute-start(bf16[256,8,64]{0,2,1:T(8,128)(2,1)S(1)} %pad_maximum_fusion.1), channel_id=1, source_target_pairs={{0,1},{2,3},{4,5},{6,7},{8,9},{10,11},{12,13},{14,15},{16,17},{18,... | collective-permute-start | bytes 786440 | tf_op jit(solution)/shard_map/ppermute | solution.py:13
  26.2 7.5 %collective-permute-start = (bf16[256,8,64]{0,2,1:T(8,128)(2,1)S(1)}, bf16[256,8,64]{0,2,1:T(8,128)(2,1)}, u32[]{:S(2)}, u32[]{:S(2)}) collective-permute-start(bf16[256,8,64]{0,2,1:T(8,128)(2,1)S(1)} %fusion.102), channel_id=1, source_target_pairs={{0,1},{2,3},{4,5},{6,7},{8,9},{10,11},{12,13},{14,15},{16,17},{18,... | collective-permute-start | bytes 786440 | tf_op jit(solution)/shard_map/ppermute | solution.py:13
  35.9 2.3 copy-start.9
  35.9 2.9 copy-start.6
  37.8 58.2 %copy-start.3 = (bf16[1,256,2304]{2,1,0:T(8,128)(2,1)S(1)}, bf16[1,256,2304]{2,1,0:T(8,128)(2,1)}, u32[]{:S(2)}) copy-start(bf16[1,256,2304]{2,1,0:T(8,128)(2,1)} %param.15) | copy-start | bytes 3538948
  37.8 59.9 %copy-start.7 = (f32[2304]{0:T(1024)S(1)}, f32[2304]{0:T(1024)}, u32[]{:S(2)}) copy-start(f32[2304]{0:T(1024)} %param.19) | copy-start | bytes 27652
  37.8 264.8 %reduce-scatter.2.cloned.1.call-start = ((), (), s32[]{:S(2)}) async-start(), calls=%async_computation.8 | async-start | bytes 1474560 | tf_op jit(solution)/shard_map/reduce_scatter | solution.py:172
  98.3 9.2 %copy-start.5 = (bf16[1,16,64,2,512]{4,3,2,1,0:T(2,128)(2,1)S(1)}, bf16[1,16,64,2,512]{4,3,2,1,0:T(2,128)(2,1)}, u32[]{:S(2)}) copy-start(bf16[1,16,64,2,512]{4,3,2,1,0:T(2,128)(2,1)} %param.24) | copy-start | bytes 6291460
  103.7 22.1 %collective-permute-start.2 = (bf16[192,1,2304]{2,0,1:T(8,128)(2,1)}, bf16[192,1,2304]{2,0,1:T(8,128)(2,1)}, u32[]{:S(2)}, u32[]{:S(2)}) collective-permute-start(bf16[192,1,2304]{2,0,1:T(8,128)(2,1)} %bitcast.36), channel_id=1, source_target_pairs={{0,8},{8,0},{16,24},{24,16},{1,9},{9,1},{17,25},{25,17},{2,10},{10... | collective-permute-start | bytes 2654216 | tf_op jit(solution)/shard_map/ppermute | solution.py:134
  105.2 21.8 %collective-permute-start.3 = (bf16[192,1,2304]{2,0,1:T(8,128)(2,1)}, bf16[192,1,2304]{2,0,1:T(8,128)(2,1)}, u32[]{:S(2)}, u32[]{:S(2)}) collective-permute-start(bf16[192,1,2304]{2,0,1:T(8,128)(2,1)} %bitcast.36), channel_id=1, source_target_pairs={{0,16},{8,24},{16,0},{24,8},{1,17},{9,25},{17,1},{25,9},{2,18},{10... | collective-permute-start | bytes 2654216 | tf_op jit(solution)/shard_map/ppermute | solution.py:134
  127.0 11.7 %slice-start.2 = ((s8[13271040]{0:T(1024)(128)(4,1)}), s8[4194304]{0:T(1024)(128)(4,1)S(1)}, s32[]{:S(2)}) async-start(s8[13271040]{0:T(1024)(128)(4,1)} %bitcast.197), calls=%async_computation.11 | async-start | bytes 8388608
  128.7 10.0 %slice-start.3 = ((s8[13271040]{0:T(1024)(128)(4,1)}), s8[4194304]{0:T(1024)(128)(4,1)S(1)}, s32[]{:S(2)}) async-start(s8[13271040]{0:T(1024)(128)(4,1)} %bitcast.197), calls=%async_computation.12 | async-start | bytes 8388608
  128.7 10.0 %slice-start.4 = ((s8[13271040]{0:T(1024)(128)(4,1)}), s8[4194304]{0:T(1024)(128)(4,1)S(1)}, s32[]{:S(2)}) async-start(s8[13271040]{0:T(1024)(128)(4,1)} %bitcast.197), calls=%async_computation.13 | async-start | bytes 8388608
  128.8 10.0 %slice-start.5 = ((s8[13271040]{0:T(1024)(128)(4,1)}), s8[688128]{0:T(1024)(128)(4,1)S(1)}, s32[]{:S(2)}) async-start(s8[13271040]{0:T(1024)(128)(4,1)} %bitcast.197), calls=%async_computation.14 | async-start | bytes 1376256
  143.1 32.1 %collective-permute-start.4 = (bf16[192,1,2304]{2,0,1:T(8,128)(2,1)}, bf16[192,1,2304]{2,0,1:T(8,128)(2,1)}, u32[]{:S(2)}, u32[]{:S(2)}) collective-permute-start(bf16[192,1,2304]{2,0,1:T(8,128)(2,1)} %get-tuple-element.18), channel_id=1, source_target_pairs={{0,8},{8,0},{16,24},{24,16},{1,9},{9,1},{17,25},{25,17},{2,10},{10... | collective-permute-start | bytes 2654216 | tf_op jit(solution)/shard_map/ppermute | solution.py:134
  143.6 48.5 %collective-permute-start.5 = (bf16[192,1,2304]{2,0,1:T(8,128)(2,1)}, bf16[192,1,2304]{2,0,1:T(8,128)(2,1)}, u32[]{:S(2)}, u32[]{:S(2)}) collective-permute-start(bf16[192,1,2304]{2,0,1:T(8,128)(2,1)} %get-tuple-element.17), channel_id=1, source_target_pairs={{0,16},{8,24},{16,0},{24,8},{1,17},{9,25},{17,1},{25,9},{2,18},{10... | collective-permute-start | bytes 2654216 | tf_op jit(solution)/shard_map/ppermute | solution.py:134
  145.1 63.1 %collective-permute-start.6 = (bf16[192,1,2304]{2,0,1:T(8,128)(2,1)}, bf16[192,1,2304]{2,0,1:T(8,128)(2,1)}, u32[]{:S(2)}, u32[]{:S(2)}) collective-permute-start(bf16[192,1,2304]{2,0,1:T(8,128)(2,1)} %collective-permute-done.2), channel_id=1, source_target_pairs={{0,16},{8,24},{16,0},{24,8},{1,17},{9,25},{17,1},{25,9},{2,18},{10... | collective-permute-start | bytes 2654216 | tf_op jit(solution)/shard_map/ppermute | solution.py:134
  206.4 10.2 %slice-start.6 = ((s8[13271040]{0:T(1024)(128)(4,1)}), s8[4194304]{0:T(1024)(128)(4,1)S(1)}, s32[]{:S(2)}) async-start(s8[13271040]{0:T(1024)(128)(4,1)} %bitcast.199), calls=%async_computation.15 | async-start | bytes 8388608
  206.4 14.9 %slice-start = ((s8[4718592]{0:T(1024)(128)(4,1)}), s8[4194304]{0:T(1024)(128)(4,1)S(1)}, s32[]{:S(2)}) async-start(s8[4718592]{0:T(1024)(128)(4,1)} %bitcast.184), calls=%async_computation.9 | async-start | bytes 8388608
  208.2 8.4 %slice-start.7 = ((s8[13271040]{0:T(1024)(128)(4,1)}), s8[4194304]{0:T(1024)(128)(4,1)S(1)}, s32[]{:S(2)}) async-start(s8[13271040]{0:T(1024)(128)(4,1)} %bitcast.199), calls=%async_computation.16 | async-start | bytes 8388608
  208.2 8.9 %slice-start.8 = ((s8[13271040]{0:T(1024)(128)(4,1)}), s8[4194304]{0:T(1024)(128)(4,1)S(1)}, s32[]{:S(2)}) async-start(s8[13271040]{0:T(1024)(128)(4,1)} %bitcast.199), calls=%async_computation.17 | async-start | bytes 8388608
  208.2 9.0 %slice-start.9 = ((s8[13271040]{0:T(1024)(128)(4,1)}), s8[688128]{0:T(1024)(128)(4,1)S(1)}, s32[]{:S(2)}) async-start(s8[13271040]{0:T(1024)(128)(4,1)} %bitcast.199), calls=%async_computation.18 | async-start | bytes 1376256
  208.2 13.1 %slice-start.1 = ((s8[4718592]{0:T(1024)(128)(4,1)}), s8[524288]{0:T(1024)(128)(4,1)S(1)}, s32[]{:S(2)}) async-start(s8[4718592]{0:T(1024)(128)(4,1)} %bitcast.184), calls=%async_computation.10 | async-start | bytes 1048576
  217.2 4.2 %copy-start.4 = (bf16[192,1,2304]{2,0,1:T(8,128)(2,1)S(1)}, bf16[192,1,2304]{2,0,1:T(8,128)(2,1)}, u32[]{:S(2)}) copy-start(bf16[192,1,2304]{2,0,1:T(8,128)(2,1)} %copy.65) | copy-start | bytes 2654212
  218.9 22.8 %collective-permute-start.7 = (bf16[192,1,2304]{2,0,1:T(8,128)(2,1)S(1)}, bf16[192,1,2304]{2,0,1:T(8,128)(2,1)}, u32[]{:S(2)}, u32[]{:S(2)}) collective-permute-start(bf16[192,1,2304]{2,0,1:T(8,128)(2,1)S(1)} %fusion.39), channel_id=1, source_target_pairs={{0,24},{8,16},{16,8},{24,0},{1,25},{9,17},{17,9},{25,1},{2,26},{10... | collective-permute-start | bytes 2654216 | tf_op jit(solution)/shard_map/ppermute | solution.py:134
  266.0 3.9 %copy-start.8 = (s32[4,16]{1,0:T(4,128)S(1)}, s32[4,16]{1,0:T(4,128)}, u32[]{:S(2)}) copy-start(s32[4,16]{1,0:T(4,128)} %param.27) | copy-start | bytes 772
  266.0 29.2 %all-to-all-start.5 = ((bf16[16,64,2,512]{3,1,2,0:T(8,128)(2,1)}), bf16[16,64,2,512]{3,1,2,0:T(8,128)(2,1)S(1)}, u32[]{:S(2)}, u32[]{:S(2)}) async-start(bf16[16,64,2,512]{3,1,2,0:T(8,128)(2,1)} %broadcast_select_fusion.1), calls=%async_computation.6 | async-start | bytes 4194304 | tf_op jit(solution)/shard_map/all_to_all | solution.py:208
  297.1 7.2 %copy-start.1 = (bf16[512,2304]{1,0:T(8,128)(2,1)S(1)}, bf16[512,2304]{1,0:T(8,128)(2,1)}, u32[]{:S(2)}) copy-start(bf16[512,2304]{1,0:T(8,128)(2,1)} %param.18) | copy-start | bytes 7077892
Sparse Core Ops, SparseCore 0:
  37.9 57.9 all-reduce.1
  264.5 28.7 reduce-scatter.1
where the time goes:
time: 313 us; the launch traced here: 311 us
  waiting for transfers between devices  113 us (36%)
  matrix products  55.9 us (18%)
  local copies, waits for them, and re-layouts  52.6 us (17%)
  blocking collectives  31.1 us (10%)
  other arithmetic  27.7 us (9%)
  starting transfers between devices  16.9 us (5%)
  between operations  14.5 us (5%)
    psum x1, waiting for transfers between devices, body(): lax.psum(partial_value.astype(jnp.bfloat16), 'head').astype(jnp.float32)  55.2 us
    unnamed x54, local copies, waits for them, and re-layouts  40.4 us
    ppermute x6, waiting for transfers between devices, partner_move(): return lax.ppermute(block, 'req', [(i, i ^ step) for i in range(req_total)])  32.2 us
    dot_general x3, matrix products, experts_on(): jnp.einsum('ned,egdf->gnef', flat, gate_up_here, preferred_element_type=j...  25.9 us
    all_to_all x4, blocking collectives, body(): part = lax.all_to_all(part, 'dev', split_axis=0, concat_axis=1, tiled=True)  25.8 us
    all_to_all x1, waiting for transfers between devices, body(): lax.all_to_all(outgoing, 'req', split_axis=0, concat_axis=0, tiled=True)  25.1 us
    dot_general x4, matrix products, body(): jnp.einsum('tec,ced->ted', dispatch_bf, part, preferred_element_type=jnp....  11.2 us
    ppermute x3, other arithmetic, partner_move(): return lax.ppermute(block, 'req', [(i, i ^ step) for i in range(req_total)])  9.36 us
  transfers between devices with their start and end apart: 11, of which 5 were waited for; matrix products, arithmetic and copies ran while one was open for 22% of the time, Pallas kernels for 0%

commit v1 on v0

--- a/solution.py
+++ b/solution.py
@@ -158,7 +158,12 @@
             part = outs[slot_index]
             part = part if step == 0 else partner_move(part, step)
             if split:
-                part = lax.all_to_all(part, "dev", split_axis=0, concat_axis=1, tiled=True)
+                part = jnp.concatenate(
+                    lax.all_to_all(
+                        jnp.stack(jnp.split(part, lax.axis_size("dev"), axis=0)), "dev", 0, 0
+                    ),
+                    axis=1,
+                )
             returned.append(part)
     token_weights = jnp.sum(own_combine, axis=-1)
     dispatch_bf = own_dispatch.astype(jnp.bfloat16)

time: 313 us -> 270 us (0.86)
  local copies, waits for them, and re-layouts: 52.6 us -> 28.2 us
  blocking collectives: 31.1 us -> 13.5 us
  other arithmetic: 27.7 us -> 17.8 us
  starting transfers between devices: 16.9 us -> 24.9 us
    unnamed x54 -> x28, local copies, waits for them, and re-layouts: 40.4 us -> 14.4 us
    all_to_all x4 -> x2, blocking collectives: 25.8 us -> 8.85 us  [body(): lax.all_to_all(jnp.stack(jnp.split(part, lax.axis_size('dev'), axis=0)),...]
    ppermute x3 -> x0, other arithmetic: 9.36 us -> none  [partner_move(): return lax.ppermute(block, 'req', [(i, i ^ step) for i in range(req_total)])]
    all_to_all x0 -> x2, starting transfers between devices: none -> 8.93 us  [body(): lax.all_to_all(jnp.stack(jnp.split(part, lax.axis_size('dev'), axis=0)),...]
    ppermute x6, waiting for transfers between devices: 32.2 us -> 37.9 us  [partner_move(): return lax.ppermute(block, 'req', [(i, i ^ step) for i in range(req_total)])]
    psum x1, waiting for transfers between devices: 55.2 us -> 49.4 us  [body(): lax.psum(partial_value.astype(jnp.bfloat16), 'head').astype(jnp.float32)]
    convert_element_type x1 -> x0, other arithmetic: 3.13 us -> none  [experts_on(): return down.astype(jnp.bfloat16).reshape(rows.shape)]
  transfers between devices with their start and end apart: 11 -> 13, of which waited for: 5 -> 6; matrix products, arithmetic and copies ran while one was open for 22% -> 23% of each run, Pallas kernels for 0% -> 0%
where the time goes in v1:
time: 270 us; the launch traced here: 269 us
  waiting for transfers between devices  113 us (42%)
  matrix products  57.4 us (21%)
  local copies, waits for them, and re-layouts  28.2 us (10%)
  starting transfers between devices  24.9 us (9%)
  other arithmetic  17.8 us (7%)
  between operations  14.5 us (5%)
  blocking collectives  13.5 us (5%)
    psum x1, waiting for transfers between devices, body(): lax.psum(partial_value.astype(jnp.bfloat16), 'head').astype(jnp.float32)  49.4 us
    ppermute x6, waiting for transfers between devices, partner_move(): return lax.ppermute(block, 'req', [(i, i ^ step) for i in range(req_total)])  37.9 us
    all_to_all x1, waiting for transfers between devices, body(): lax.all_to_all(outgoing, 'req', split_axis=0, concat_axis=0, tiled=True)  25.1 us
    dot_general x3, matrix products, experts_on(): jnp.einsum('ned,egdf->gnef', flat, gate_up_here, preferred_element_type=j...  24.7 us
    unnamed x28, local copies, waits for them, and re-layouts  14.4 us
    dot_general x4, matrix products, body(): jnp.einsum('tec,ced->ted', dispatch_bf, part, preferred_element_type=jnp....  13.9 us
    all_to_all x2, starting transfers between devices, body(): lax.all_to_all(jnp.stack(jnp.split(part, lax.axis_size('dev'), axis=0)),...  8.93 us
    all_to_all x2, blocking collectives, body(): lax.all_to_all(jnp.stack(jnp.split(part, lax.axis_size('dev'), axis=0)),...  8.85 us
  transfers between devices with their start and end apart: 13, of which 6 were waited for; matrix products, arithmetic and copies ran while one was open for 23% of the time, Pallas kernels for 0%

profile of v1, /device:TPU:0, one launch (start us, length us, event | category | flops | bytes accessed | tf_op | source)
XLA Modules:
  0.0 268.8 jit_solution(8197546861257384548)
XLA Ops:
  7.3 10.3 %copy.37 = bf16[2304,3,512]{0,2,1:T(8,128)(2,1)} copy(bf16[2304,3,512]{2,0,1:T(8,128)(2,1)} %param.17) | data formatting | bytes 14155776 | tf_op args[2]
  17.9 5.2 %fusion.68 = f32[256,3,8,64]{0,3,2,1:T(8,128)S(1)} fusion(bf16[3,8,64,2304]{3,2,1,0:T(8,128)(2,1)} %bitcast.196, bf16[1,256,2304]{2,1,0:T(8,128)(2,1)S(1)} %copy-done.2, f32[2304]{0:T(1024)} %param.16, f32[256]{0:T(256)S(1)} %add_rsqrt_fusion.1), kind=kOutput, calls=%fused_computation.64 | convolution fusion | flops 1814298624 | bytes 9840640 | tf_op jit(solution)/shard_map/dot_general | solution.py:73
  23.5 3.1 %collective-permute-start.1 = (bf16[256,8,64]{0,2,1:T(8,128)(2,1)S(1)}, bf16[256,8,64]{0,2,1:T(8,128)(2,1)}, u32[]{:S(2)}, u32[]{:S(2)}) collective-permute-start(bf16[256,8,64]{0,2,1:T(8,128)(2,1)S(1)} %pad_maximum_fusion.5), channel_id=1, source_target_pairs={{0,1},{2,3},{4,5},{6,7},{8,9},{10,11},{12,13},{14,15},{16,17},{18,... | collective-permute-start | bytes 786440 | tf_op jit(solution)/shard_map/ppermute | solution.py:13
  26.6 2.0 collective-permute-start
  32.0 1.9 fusion.35
  33.8 1.3 fusion.42
  35.2 2.1 fusion.83
  37.3 1.8 convolution_convert_fusion
  40.9 3.2 %bitcast_select_fusion = bf16[16,64,2,512]{3,1,2,0:T(8,128)(2,1)} fusion(bf16[1,16,64,2,512]{4,3,2,1,0:T(2,128)(2,1)} %param.24, pred[16,64]{1,0:T(8,128)(4,1)S(1)} %add_compare_fusion), kind=kLoop, calls=%fused_computation.55 | loop fusion | flops 1048576 | bytes 4195328 | tf_op jit(solution)/shard_map/jit(_where)/select_n | solution.py:209
  44.1 2.3 gather_fusion
  47.9 49.4 %all-reduce.2.cloned.1.call-done = bf16[256,2304]{1,0:T(8,128)(2,1)} async-done(((bf16[256,2304]{1,0:T(8,128)(2,1)}), bf16[256,2304]{1,0:T(8,128)(2,1)}) %all-reduce.2.cloned.1.call-update) | async-done | bytes 1179664 | tf_op jit(solution)/shard_map/psum | solution.py:104
  97.3 2.1 fusion.52
  100.1 4.7 %all_to_all.43 = bf16[96,2,2304]{2,0,1:T(8,128)(2,1)S(1)} all-to-all(bf16[96,2,2304]{2,0,1:T(8,128)(2,1)S(1)} %convert_bitcast_fusion.1), channel_id=1, replica_groups=mesh['req'=4,'head'=4,'dev'=2] {'dev'}, dimensions={1} | all-to-all | bytes 1769472 | tf_op jit(solution)/shard_map/all_to_all | solution.py:129
  104.8 1.5 collective-permute-start.2
  106.3 1.5 collective-permute-start.3
  107.8 7.6 %fusion.44 = f32[2,192,1,1440]{3,1,0,2:T(8,128)S(1)} fusion(bf16[192,2304,1]{1,0,2:T(8,128)(2,1)S(1)} %bitcast.204, bf16[2,2,2304,1440]{2,3,1,0:T(8,128)(2,1)} %param.22, s32[]{:T(128)S(6)} %select_n.44), kind=kOutput, calls=%fused_computation.38 | convolution fusion | flops 2548039680 | bytes 16367620 | tf_op jit(solution)/shard_map/ned,egdf->gnef/dot_general | solution.py:139
  115.4 1.7 fusion.36
  117.2 4.4 %all_to_all.44 = bf16[2,96,1,2304]{3,1,2,0:T(8,128)(2,1)S(1)} all-to-all(bf16[2,96,1,2304]{3,1,2,0:T(8,128)(2,1)S(1)} %pad_maximum_fusion.1), channel_id=1, replica_groups=mesh['req'=4,'head'=4,'dev'=2] {'dev'}, dimensions={0} | all-to-all | bytes 1769472 | tf_op jit(solution)/shard_map/all_to_all | solution.py:162
  121.7 2.9 %fusion.89 = f32[2,2304,256]{2,1,0:T(8,128)} fusion(bf16[256,2,96]{0,2,1:T(8,128)(2,1)S(1)} %get-tuple-element.12, bf16[2,96,1,2304]{3,1,2,0:T(8,128)(2,1)S(1)} %all_to_all.44), kind=kOutput, calls=%fused_computation.84 | convolution fusion | flops 226492416 | bytes 5701632 | tf_op jit(solution)/shard_map/tec,ced->ted/dot_general | solution.py:172
  124.6 2.0 collective-permute-done.2
  126.6 1.2 collective-permute-done.3
  127.9 9.7 %fusion.26 = f32[2,384,1,1440]{1,3,0,2:T(8,128)S(1)} fusion(bf16[384,2304,1]{1,0,2:T(8,128)(2,1)S(1)} %bitcast.199, bf16[2,2,2304,1440]{2,3,1,0:T(8,128)(2,1)} %param.22, s32[]{:T(128)S(6)} %select_n.44), kind=kOutput, calls=%fused_computation.30 | convolution fusion | flops 5096079360 | bytes 19464196 | tf_op jit(solution)/shard_map/ned,egdf->gnef/dot_general | solution.py:139
  137.6 1.5 collective-permute-start.6
  139.2 3.0 %fusion.23 = bf16[384,1,2304]{2,0,1:T(8,128)(2,1)S(1)} fusion(bf16[2,1440,2304]{2,1,0:T(8,128)(2,1)S(1)} %bitcast.209, s32[]{:T(128)S(6)} %select_n.44, f32[2,384,1,1440]{1,3,0,2:T(8,128)S(1)} %fusion.26), kind=kOutput, calls=%fused_computation.28 | convolution fusion | flops 2552242176 | bytes 12828676 | tf_op jit(solution)/shard_map/nef,efd->ned/dot_general | solution.py:141
  142.2 1.0 fusion.132
  144.3 16.0 %collective-permute-done.6 = bf16[192,1,2304]{2,0,1:T(8,128)(2,1)S(1)} collective-permute-done((bf16[192,1,2304]{2,0,1:T(8,128)(2,1)S(1)}, bf16[192,1,2304]{2,0,1:T(8,128)(2,1)S(1)}, u32[]{:S(2)}, u32[]{:S(2)}) %collective-permute-start.6) | collective-permute-done | bytes 884768 | tf_op jit(solution)/shard_map/ppermute | solution.py:134
  160.3 7.4 %fusion.47 = f32[2,192,1,1440]{3,1,0,2:T(8,128)S(1)} fusion(bf16[2,2,2304,1440]{2,3,1,0:T(8,128)(2,1)} %param.22, s32[]{:T(128)S(6)} %select_n.44, bf16[192,1,2304]{2,0,1:T(8,128)(2,1)S(1)} %collective-permute-done.6), kind=kOutput, calls=%fused_computation.39 | convolution fusion | flops 2548039680 | bytes 16367620 | tf_op jit(solution)/shard_map/ned,egdf->gnef/dot_general | solution.py:139
  167.7 2.6 fusion.39
  170.3 1.5 collective-permute-start.7
  171.9 1.0 pad_maximum_fusion.2
  172.9 4.6 %all-to-all-start.2 = ((bf16[2,96,1,2304]{3,1,2,0:T(8,128)(2,1)}), bf16[2,96,1,2304]{3,1,2,0:T(8,128)(2,1)}, u32[]{:S(2)}, u32[]{:S(2)}) async-start(bf16[2,96,1,2304]{3,1,2,0:T(8,128)(2,1)} %pad_maximum_fusion.2), calls=%async_computation.2 | async-start | bytes 1769472 | tf_op jit(solution)/shard_map/all_to_all | solution.py:162
  177.5 18.8 %collective-permute-done.5 = bf16[192,1,2304]{2,0,1:T(8,128)(2,1)} collective-permute-done((bf16[192,1,2304]{2,0,1:T(8,128)(2,1)}, bf16[192,1,2304]{2,0,1:T(8,128)(2,1)}, u32[]{:S(2)}, u32[]{:S(2)}) %collective-permute-start.5) | collective-permute-done | bytes 884768 | tf_op jit(solution)/shard_map/ppermute | solution.py:134
  196.3 1.2 slice_bitcast_fusion.5
  197.5 1.0 pad_maximum_fusion.3
  198.5 4.3 %all-to-all-start.3 = ((bf16[2,96,1,2304]{3,1,2,0:T(8,128)(2,1)}), bf16[2,96,1,2304]{3,1,2,0:T(8,128)(2,1)}, u32[]{:S(2)}, u32[]{:S(2)}) async-start(bf16[2,96,1,2304]{3,1,2,0:T(8,128)(2,1)} %pad_maximum_fusion.3), calls=%async_computation.3 | async-start | bytes 1769472 | tf_op jit(solution)/shard_map/all_to_all | solution.py:162
  202.9 5.6 %convolution_add_fusion.2 = f32[2,2304,256]{2,1,0:T(8,128)} fusion(f32[2,2304,256]{2,1,0:T(8,128)} %fusion.89, bf16[256,2,96]{0,2,1:T(8,128)(2,1)S(1)} %get-tuple-element.12, bf16[2,96,1,2304]{3,1,2,0:T(8,128)(2,1)} %all-to-all-done.2), kind=kOutput, calls=%fused_computation.19 | convolution fusion | flops 227672064 | bytes 10420224 | tf_op jit(solution)/shard_map/tec,ced->ted/dot_general | solution.py:172
  208.5 3.4 %convolution_add_fusion.1 = f32[2,2304,256]{2,1,0:T(8,128)S(1)} fusion(f32[2,2304,256]{2,1,0:T(8,128)} %convolution_add_fusion.2, bf16[256,2,96]{0,2,1:T(8,128)(2,1)S(1)} %get-tuple-element.12, bf16[2,96,1,2304]{3,1,2,0:T(8,128)(2,1)} %all-to-all-done.3), kind=kOutput, calls=%fused_computation.18 | convolution fusion | flops 227672064 | bytes 10420224 | tf_op jit(solution)/shard_map/tec,ced->ted/dot_general | solution.py:172
  212.0 1.2 slice_bitcast_fusion.3
  213.3 4.4 %all_to_all.45 = bf16[2,96,1,2304]{3,1,2,0:T(8,128)(2,1)S(1)} all-to-all(bf16[2,96,1,2304]{3,1,2,0:T(8,128)(2,1)S(1)} %pad_maximum_fusion.4), channel_id=1, replica_groups=mesh['req'=4,'head'=4,'dev'=2] {'dev'}, dimensions={0} | all-to-all | bytes 1769472 | tf_op jit(solution)/shard_map/all_to_all | solution.py:162
  217.7 1.9 fusion.63
  219.6 2.4 copy.40
  222.0 1.6 broadcast_select_fusion.1
  223.6 3.8 %all-to-all-start.5 = ((bf16[16,64,2,512]{3,1,2,0:T(8,128)(2,1)}), bf16[16,64,2,512]{3,1,2,0:T(8,128)(2,1)S(1)}, u32[]{:S(2)}, u32[]{:S(2)}) async-start(bf16[16,64,2,512]{3,1,2,0:T(8,128)(2,1)} %broadcast_select_fusion.1), calls=%async_computation.6 | async-start | bytes 4194304 | tf_op jit(solution)/shard_map/all_to_all | solution.py:213
  227.6 25.1 %all-to-all-done.5 = bf16[16,64,2,512]{3,1,2,0:T(8,128)(2,1)S(1)} async-done(((bf16[16,64,2,512]{3,1,2,0:T(8,128)(2,1)}), bf16[16,64,2,512]{3,1,2,0:T(8,128)(2,1)S(1)}, u32[]{:S(2)}, u32[]{:S(2)}) %all-to-all-start.5) | async-done | bytes 2097184 | tf_op jit(solution)/shard_map/all_to_all | solution.py:213
  252.8 2.0 gather_fusion.1
  254.8 2.0 broadcast_select_fusion
  256.8 3.5 %copy.42 = bf16[16,64,2,512]{3,2,1,0:T(2,128)(2,1)} copy(bf16[16,64,2,512]{3,1,2,0:T(8,128)(2,1)S(1)} %broadcast_select_fusion) | data formatting | bytes 4194304
  260.3 1.7 fusion.106
  (98 shorter events, 9.8 us)
Async XLA Ops:
  7.2 30.2 %copy-start = (bf16[512,2304]{1,0:T(8,128)(2,1)S(1)}, bf16[512,2304]{1,0:T(8,128)(2,1)}, u32[]{:S(2)}) copy-start(bf16[512,2304]{1,0:T(8,128)(2,1)} %param.18) | copy-start | bytes 7077892
  7.2 90.2 %all-reduce.2.cloned.1.call-start = ((), (), s32[]{:S(2)}) async-start(), calls=%async_computation.7 | async-start | bytes 2359296 | tf_op jit(solution)/shard_map/psum | solution.py:104
  7.3 10.3 %copy-start.2 = (bf16[1,256,2304]{2,1,0:T(8,128)(2,1)S(1)}, bf16[1,256,2304]{2,1,0:T(8,128)(2,1)}, u32[]{:S(2)}) copy-start(bf16[1,256,2304]{2,1,0:T(8,128)(2,1)} %param.15) | copy-start | bytes 3538948
  23.1 7.7 %copy-start.3 = (s32[4,16]{1,0:T(4,128)S(1)}, s32[4,16]{1,0:T(4,128)}, u32[]{:S(2)}) copy-start(s32[4,16]{1,0:T(4,128)} %param.26) | copy-start | bytes 772
  23.5 8.4 %collective-permute-start.1 = (bf16[256,8,64]{0,2,1:T(8,128)(2,1)S(1)}, bf16[256,8,64]{0,2,1:T(8,128)(2,1)}, u32[]{:S(2)}, u32[]{:S(2)}) collective-permute-start(bf16[256,8,64]{0,2,1:T(8,128)(2,1)S(1)} %pad_maximum_fusion.5), channel_id=1, source_target_pairs={{0,1},{2,3},{4,5},{6,7},{8,9},{10,11},{12,13},{14,15},{16,17},{18,... | collective-permute-start | bytes 786440 | tf_op jit(solution)/shard_map/ppermute | solution.py:13
  26.6 8.5 %collective-permute-start = (bf16[256,8,64]{0,2,1:T(8,128)(2,1)S(1)}, bf16[256,8,64]{0,2,1:T(8,128)(2,1)}, u32[]{:S(2)}, u32[]{:S(2)}) collective-permute-start(bf16[256,8,64]{0,2,1:T(8,128)(2,1)S(1)} %fusion.107), channel_id=1, source_target_pairs={{0,1},{2,3},{4,5},{6,7},{8,9},{10,11},{12,13},{14,15},{16,17},{18,... | collective-permute-start | bytes 786440 | tf_op jit(solution)/shard_map/ppermute | solution.py:13
  31.1 0.6 copy-start.7
  37.3 2.2 copy-start.6
  46.4 53.1 %copy-start.4 = (f32[2304]{0:T(1024)S(1)}, f32[2304]{0:T(1024)}, u32[]{:S(2)}) copy-start(f32[2304]{0:T(1024)} %param.19) | copy-start | bytes 27652
  100.1 15.2 %slice-start = ((s8[13271040]{0:T(1024)(128)(4,1)}), s8[4194304]{0:T(1024)(128)(4,1)S(1)}, s32[]{:S(2)}) async-start(s8[13271040]{0:T(1024)(128)(4,1)} %bitcast.208), calls=%async_computation.9 | async-start | bytes 8388608
  104.8 21.7 %collective-permute-start.2 = (bf16[192,1,2304]{2,0,1:T(8,128)(2,1)S(1)}, bf16[192,1,2304]{2,0,1:T(8,128)(2,1)S(1)}, u32[]{:S(2)}, u32[]{:S(2)}) collective-permute-start(bf16[192,1,2304]{2,0,1:T(8,128)(2,1)S(1)} %bitcast.202), channel_id=1, source_target_pairs={{0,8},{8,0},{16,24},{24,16},{1,9},{9,1},{17,25},{25,17},{2,10},{10... | collective-permute-start | bytes 2654216 | tf_op jit(solution)/shard_map/ppermute | solution.py:134
  106.3 21.5 %collective-permute-start.3 = (bf16[192,1,2304]{2,0,1:T(8,128)(2,1)S(1)}, bf16[192,1,2304]{2,0,1:T(8,128)(2,1)S(1)}, u32[]{:S(2)}, u32[]{:S(2)}) collective-permute-start(bf16[192,1,2304]{2,0,1:T(8,128)(2,1)S(1)} %bitcast.203), channel_id=1, source_target_pairs={{0,16},{8,24},{16,0},{24,8},{1,17},{9,25},{17,1},{25,9},{2,18},{10... | collective-permute-start | bytes 2654216 | tf_op jit(solution)/shard_map/ppermute | solution.py:134
  107.8 7.6 %slice-start.1 = ((s8[13271040]{0:T(1024)(128)(4,1)}), s8[4194304]{0:T(1024)(128)(4,1)S(1)}, s32[]{:S(2)}) async-start(s8[13271040]{0:T(1024)(128)(4,1)} %bitcast.208), calls=%async_computation.10 | async-start | bytes 8388608
  107.8 7.6 %slice-start.2 = ((s8[13271040]{0:T(1024)(128)(4,1)}), s8[4194304]{0:T(1024)(128)(4,1)S(1)}, s32[]{:S(2)}) async-start(s8[13271040]{0:T(1024)(128)(4,1)} %bitcast.208), calls=%async_computation.11 | async-start | bytes 8388608
  107.8 7.6 %slice-start.3 = ((s8[13271040]{0:T(1024)(128)(4,1)}), s8[688128]{0:T(1024)(128)(4,1)S(1)}, s32[]{:S(2)}) async-start(s8[13271040]{0:T(1024)(128)(4,1)} %bitcast.208), calls=%async_computation.12 | async-start | bytes 1376256
  137.6 22.7 %collective-permute-start.6 = (bf16[192,1,2304]{2,0,1:T(8,128)(2,1)S(1)}, bf16[192,1,2304]{2,0,1:T(8,128)(2,1)S(1)}, u32[]{:S(2)}, u32[]{:S(2)}) collective-permute-start(bf16[192,1,2304]{2,0,1:T(8,128)(2,1)S(1)} %collective-permute-done.2), channel_id=1, source_target_pairs={{0,16},{8,24},{16,0},{24,8},{1,17},{9,25},{17,1},{25,9},{2,18},{10... | collective-permute-start | bytes 2654216 | tf_op jit(solution)/shard_map/ppermute | solution.py:134
  143.2 53.1 %collective-permute-start.5 = (bf16[192,1,2304]{2,0,1:T(8,128)(2,1)}, bf16[192,1,2304]{2,0,1:T(8,128)(2,1)}, u32[]{:S(2)}, u32[]{:S(2)}) collective-permute-start(bf16[192,1,2304]{2,0,1:T(8,128)(2,1)} %get-tuple-element.15), channel_id=1, source_target_pairs={{0,16},{8,24},{16,0},{24,8},{1,17},{9,25},{17,1},{25,9},{2,18},{10... | collective-permute-start | bytes 2654216 | tf_op jit(solution)/shard_map/ppermute | solution.py:134
  143.8 28.1 %collective-permute-start.4 = (bf16[192,1,2304]{2,0,1:T(8,128)(2,1)S(1)}, bf16[192,1,2304]{2,0,1:T(8,128)(2,1)S(1)}, u32[]{:S(2)}, u32[]{:S(2)}) collective-permute-start(bf16[192,1,2304]{2,0,1:T(8,128)(2,1)S(1)} %get-tuple-element.16), channel_id=1, source_target_pairs={{0,8},{8,0},{16,24},{24,16},{1,9},{9,1},{17,25},{25,17},{2,10},{10... | collective-permute-start | bytes 2654216 | tf_op jit(solution)/shard_map/ppermute | solution.py:134
  170.3 41.6 %collective-permute-start.7 = (bf16[192,1,2304]{2,0,1:T(8,128)(2,1)}, bf16[192,1,2304]{2,0,1:T(8,128)(2,1)}, u32[]{:S(2)}, u32[]{:S(2)}) collective-permute-start(bf16[192,1,2304]{2,0,1:T(8,128)(2,1)} %fusion.39), channel_id=1, source_target_pairs={{0,24},{8,16},{16,8},{24,0},{1,25},{9,17},{17,9},{25,1},{2,26},{10... | collective-permute-start | bytes 2654216 | tf_op jit(solution)/shard_map/ppermute | solution.py:134
  172.9 25.6 %all-to-all-start.2 = ((bf16[2,96,1,2304]{3,1,2,0:T(8,128)(2,1)}), bf16[2,96,1,2304]{3,1,2,0:T(8,128)(2,1)}, u32[]{:S(2)}, u32[]{:S(2)}) async-start(bf16[2,96,1,2304]{3,1,2,0:T(8,128)(2,1)} %pad_maximum_fusion.2), calls=%async_computation.2 | async-start | bytes 1769472 | tf_op jit(solution)/shard_map/all_to_all | solution.py:162
  198.5 10.0 %all-to-all-start.3 = ((bf16[2,96,1,2304]{3,1,2,0:T(8,128)(2,1)}), bf16[2,96,1,2304]{3,1,2,0:T(8,128)(2,1)}, u32[]{:S(2)}, u32[]{:S(2)}) async-start(bf16[2,96,1,2304]{3,1,2,0:T(8,128)(2,1)} %pad_maximum_fusion.3), calls=%async_computation.3 | async-start | bytes 1769472 | tf_op jit(solution)/shard_map/all_to_all | solution.py:162
  202.9 57.4 %reduce-scatter.2.cloned.1.call-start = ((), (), s32[]{:S(2)}) async-start(), calls=%async_computation.8 | async-start | bytes 1474560 | tf_op jit(solution)/shard_map/reduce_scatter | solution.py:177
  219.6 2.4 copy-start.8
  223.6 3.9 %copy-start.5 = (s32[4,16]{1,0:T(4,128)S(1)}, s32[4,16]{1,0:T(4,128)}, u32[]{:S(2)}) copy-start(s32[4,16]{1,0:T(4,128)} %param.27) | copy-start | bytes 772
  223.6 29.2 %all-to-all-start.5 = ((bf16[16,64,2,512]{3,1,2,0:T(8,128)(2,1)}), bf16[16,64,2,512]{3,1,2,0:T(8,128)(2,1)S(1)}, u32[]{:S(2)}, u32[]{:S(2)}) async-start(bf16[16,64,2,512]{3,1,2,0:T(8,128)(2,1)} %broadcast_select_fusion.1), calls=%async_computation.6 | async-start | bytes 4194304 | tf_op jit(solution)/shard_map/all_to_all | solution.py:213
  254.8 7.2 %copy-start.1 = (bf16[512,2304]{1,0:T(8,128)(2,1)S(1)}, bf16[512,2304]{1,0:T(8,128)(2,1)}, u32[]{:S(2)}) copy-start(bf16[512,2304]{1,0:T(8,128)(2,1)} %param.18) | copy-start | bytes 7077892
Sparse Core Ops, SparseCore 0:
  39.3 57.9 all-reduce.1
  222.1 27.9 reduce-scatter.1
